TPU v7x, 32 devices: a whole 2x2x4 slice. The times are simulated.
32 devices in a mesh: dp: 4 (over x, core), tensor: 8 (over z, y).
Axes of the slice: x: 2, y: 2, z: 4, core: 2. Of those that a mesh axis runs over, the one named last changes fastest.
Arguments:
- grad: bfloat16 [4, 576, 6144], P('dp', 'tensor'), as said below
- momentum: float32 [4, 576, 6144], P('dp', 'tensor'), may hold values from -6 to 6
- owner: int32 [4], replicated, may hold values from 0 to 3, each once
Outputs:
- update: bfloat16 [4, 576, 6144], P(None, 'tensor')
- new_momentum: float32 [4, 576, 6144], P('dp', 'tensor')
Inputs may be any that keep to these rules, and one draw needn't show every extreme that they name: owner names each matrix 0 to 3 exactly once. `grad`: gradient entries are finite; every matrix has full rank.
All inputs are finite; a program needn't handle non-finite values.
Results may differ from a plain program's by a relative error of at most 0.0013.
The roundings to bfloat16 on the way count: a program that leaves them out, or rounds other values in their place, can miss the bound.
Values may be sent and summed in bfloat16 or wider, within the bound.
No kernel may reach another device: no remote copies, remote signals or barrier semaphores. Data moves between devices by JAX's collectives and lax.ppermute only.
A program may use at most 64 MiB of HBM per device.

v0:
```python
import math
import jax
import jax.numpy as jnp
from jax import lax
from jax.sharding import PartitionSpec as P

M = 576
N = 6144
ITERS = 2
coef_a = 3.4445
coef_b = -4.775
coef_c = 2.0315
decay = 0.95
eps = 1e-07


def per_device(grad, momentum, owner):
    new_momentum = decay * momentum + grad.astype(jnp.float32)
    direction = grad.astype(jnp.float32) + decay * new_momentum
    total = lax.psum(jnp.sum(direction * direction), "tensor")
    rows_here = (direction[0] / (jnp.sqrt(total) + eps)).astype(jnp.bfloat16)
    columns = lax.all_to_all(rows_here, "tensor", split_axis=1, concat_axis=0, tiled=True)
    for step in range(ITERS):
        gram = lax.psum(
            jnp.dot(columns, columns.T, preferred_element_type=jnp.float32), "tensor"
        ).astype(jnp.bfloat16)
        square = jnp.dot(gram, gram, preferred_element_type=jnp.float32)
        poly = (coef_b * gram.astype(jnp.float32) + coef_c * square).astype(jnp.bfloat16)
        applied = jnp.dot(poly, columns, preferred_element_type=jnp.float32)
        columns = (coef_a * columns.astype(jnp.float32) + applied).astype(jnp.bfloat16)
    factor = 0.2 * math.sqrt(max(M, N))
    back_rows = lax.all_to_all(columns, "tensor", split_axis=0, concat_axis=1, tiled=True)
    scaled = (factor * back_rows.astype(jnp.float32)).astype(jnp.bfloat16)
    every_slot = lax.all_gather(scaled[None], "dp", axis=0, tiled=True)
    matrix_ids = jnp.arange(every_slot.shape[0], dtype=jnp.int32)
    selector = (owner[None, :] == matrix_ids[:, None]).astype(jnp.bfloat16)
    update = jnp.einsum(
        "mg,grn->mrn", selector, every_slot, preferred_element_type=jnp.float32
    ).astype(jnp.bfloat16)
    return (update, new_momentum)


def solution(mesh):
    in_specs = (P("dp", "tensor", None), P("dp", "tensor", None), P())
    out_specs = (P(None, "tensor", None), P("dp", "tensor", None))
    return jax.shard_map(
        per_device, mesh=mesh, in_specs=in_specs, out_specs=out_specs, check_vma=False
    )
```

profile of v0, /device:TPU:0, one launch (start us, length us, event | category | flops | bytes accessed | tf_op | source)
XLA Modules:
  0.0 286.8 jit_solution(11792428714496908145)
XLA Ops:
  7.2 0.0 copy-start.1
  7.2 0.0 all-gather.2.cloned.1.call-start
  7.2 2.9 %multiply_reduce_fusion = (f32[]{:T(128)}, f32[1,72,6144]{2,1,0:T(8,128)S(1)}) fusion(bf16[1,72,6144]{2,1,0:T(8,128)(2,1)} %param.3, f32[1,72,6144]{2,1,0:T(8,128)} %param.4), kind=kLoop, calls=%fused_computation.8 | loop fusion | flops 3096575 | bytes 4423684 | tf_op jit(solution)/shard_map/reduce_sum | solution.py:20
  10.1 0.0 copy-start
  10.1 23.8 %psum.21 = f32[]{:T(128)} all-reduce(f32[]{:T(128)} %get-tuple-element.8), channel_id=1, replica_groups=mesh['dp'=4,'tensor'=8] {'tensor'}, use_global_device_ids=true, to_apply=%region_1.0 | all-reduce | flops 1 | bytes 8 | tf_op jit(solution)/shard_map/psum | solution.py:20
  34.6 0.0 copy-done.1
  34.6 0.3 divide_convert_fusion
  34.8 0.0 copy-done
  34.9 0.2 copy.16
  35.0 0.2 copy.12
  35.2 21.7 %all_to_all.29 = bf16[72,8,768]{2,0,1:T(8,128)(2,1)S(1)} all-to-all(bf16[72,8,768]{2,0,1:T(8,128)(2,1)S(1)} %copy.12), channel_id=1, replica_groups=mesh['dp'=4,'tensor'=8] {'tensor'}, dimensions={1} | all-to-all | bytes 1769472 | tf_op jit(solution)/shard_map/all_to_all | solution.py:22
  56.9 0.9 fusion.17
  57.7 79.9 %all-reduce.2 = bf16[576,576]{1,0:T(8,128)(2,1)S(1)} all-reduce(f32[576,576]{1,0:T(8,128)S(1)} %fusion.17), channel_id=1, replica_groups=mesh['dp'=4,'tensor'=8] {'tensor'}, use_global_device_ids=true, to_apply=%region_2.0 | all-reduce | flops 331776 | bytes 1990656 | tf_op jit(solution)/shard_map/psum | solution.py:24
  137.6 1.6 add_convert_fusion.1
  139.3 0.0 copy-start.3
  139.3 0.9 copy-done.3
  140.2 0.9 fusion.18
  141.1 0.0 copy-start.4
  141.1 78.1 %all-reduce.3 = bf16[576,576]{1,0:T(8,128)(2,1)S(1)} all-reduce(f32[576,576]{1,0:T(8,128)S(1)} %fusion.18), channel_id=1, replica_groups=mesh['dp'=4,'tensor'=8] {'tensor'}, use_global_device_ids=true, to_apply=%region_3.0 | all-reduce | flops 331776 | bytes 1990656 | tf_op jit(solution)/shard_map/psum | solution.py:24
  219.2 0.0 copy-done.4
  219.2 1.6 add_convert_fusion
  220.8 18.7 %all_to_all.30 = bf16[8,72,768]{2,1,0:T(8,128)(2,1)S(1)} all-to-all(bf16[8,72,768]{2,1,0:T(8,128)(2,1)S(1)} %bitcast.26), channel_id=1, replica_groups=mesh['dp'=4,'tensor'=8] {'tensor'}, dimensions={0} | all-to-all | bytes 1769472 | tf_op jit(solution)/shard_map/all_to_all | solution.py:32
  239.6 0.2 fusion.1
  239.7 0.2 copy.13
  239.9 0.0 copy-start.2
  239.9 1.3 convert_element_type.89
  241.2 0.0 all-gather.2.cloned.1.call-update
  241.2 28.5 %all-gather.2.cloned.1.call-done = bf16[4,72,6144]{2,1,0:T(8,128)(2,1)} async-done(((bf16[1,72,6144]{2,1,0:T(8,128)(2,1)}), bf16[4,72,6144]{2,1,0:T(8,128)(2,1)}) %all-gather.2.cloned.1.call-update) | async-done | bytes 3538960 | tf_op jit(solution)/shard_map/all_gather | solution.py:34
  269.7 0.0 copy-done.2
  269.7 6.5 %convolution_convert_fusion = bf16[4,72,6144]{2,0,1:T(4,128)(2,1)S(1)} fusion(bf16[4,72,6144]{2,1,0:T(8,128)(2,1)} %all-gather.2.cloned.1.call-done, s32[4]{0:T(128)S(1)} %copy-done.2), kind=kOutput, calls=%fused_computation | convolution fusion | flops 15925264 | bytes 7077904 | tf_op jit(solution)/shard_map/mg,grn->mrn/dot_general | solution.py:37
  276.2 3.7 %copy.15 = bf16[4,72,6144]{2,1,0:T(8,128)(2,1)} copy(bf16[4,72,6144]{2,0,1:T(4,128)(2,1)S(1)} %convolution_convert_fusion) | data formatting | bytes 7077888
Async XLA Ops:
  7.2 27.4 %copy-start.1 = (bf16[1,72,6144]{2,1,0:T(8,128)(2,1)S(1)}, bf16[1,72,6144]{2,1,0:T(8,128)(2,1)}, u32[]{:S(2)}) copy-start(bf16[1,72,6144]{2,1,0:T(8,128)(2,1)} %param.3) | copy-start | bytes 2654212
  7.2 262.5 %all-gather.2.cloned.1.call-start = ((), (), s32[]{:S(2)}) async-start(), calls=%async_computation.2 | async-start | bytes 4423680 | tf_op jit(solution)/shard_map/all_gather | solution.py:34
  10.1 24.7 %copy-start = (f32[1,72,6144]{2,1,0:T(8,128)}, f32[1,72,6144]{2,1,0:T(8,128)S(1)}, u32[]{:S(2)}) copy-start(f32[1,72,6144]{2,1,0:T(8,128)S(1)} %get-tuple-element.9) | copy-start | bytes 5308420
  139.3 0.9 copy-start.3
  141.1 78.1 %copy-start.4 = (bf16[576,768]{1,0:T(8,128)(2,1)S(1)}, bf16[576,768]{1,0:T(8,128)(2,1)}, u32[]{:S(2)}) copy-start(bf16[576,768]{1,0:T(8,128)(2,1)} %copy-done.3) | copy-start | bytes 2654212
  239.9 29.8 %copy-start.2 = (s32[4]{0:T(128)S(1)}, s32[4]{0:T(128)}, u32[]{:S(2)}) copy-start(s32[4]{0:T(128)} %param.5) | copy-start | bytes 52
Sparse Core Ops, SparseCore 0:
  241.3 28.2 all-gather.1
where the time goes:
time: 287 us
  blocking collectives  222 us (77%)
  waiting for transfers between devices  28.5 us (10%)
  between operations  14.8 us (5%)
  matrix products  11.6 us (4%)
  local copies, waits for them, and re-layouts  6.44 us (2%)
  other arithmetic  3.29 us (1%)
    psum x2, blocking collectives, per_device(): lax.psum(jnp.dot(columns, columns.T, preferred_element_type=jnp.float32),...  158 us
    all_gather x1, waiting for transfers between devices, per_device(): every_slot = lax.all_gather(scaled[None], 'dp', axis=0, tiled=True)  28.5 us
    psum x1, blocking collectives, per_device(): total = lax.psum(jnp.sum(direction * direction), 'tensor')  23.8 us
    all_to_all x1, blocking collectives, per_device(): lax.all_to_all(rows_here, 'tensor', split_axis=1, concat_axis=0, tiled=True)  21.7 us
    all_to_all x1, blocking collectives, per_device(): lax.all_to_all(columns, 'tensor', split_axis=0, concat_axis=1, tiled=True)  18.7 us
    dot_general x1, matrix products, per_device(): jnp.einsum('mg,grn->mrn', selector, every_slot, preferred_element_type=jn...  6.52 us
  transfers between devices with their start and end apart: 1, of which 1 were waited for; matrix products, arithmetic and copies ran while one was open for 0% of the time, Pallas kernels for 0%

commit v1 on v0

--- a/solution.py
+++ b/solution.py
@@ -12,6 +12,19 @@
 coef_c = 2.0315
 decay = 0.95
 eps = 1e-07
+
+
+def gather_around(x, axis, dim):
+    ways = lax.axis_size(axis)
+    up = [(d, (d + 1) % ways) for d in range(ways)]
+    down = [(d, (d - 1) % ways) for d in range(ways)]
+    earlier, later = ([x], [x])
+    for _ in range(ways // 2):
+        earlier.append(lax.ppermute(earlier[-1], axis, up))
+    for _ in range((ways - 1) // 2):
+        later.append(lax.ppermute(later[-1], axis, down))
+    line = jnp.concatenate([*earlier[::-1], *later[1:]], axis=dim)
+    return jnp.roll(line, (lax.axis_index(axis) - ways // 2) * x.shape[dim], axis=dim)
 
 
 def per_device(grad, momentum, owner):
@@ -31,7 +44,7 @@
     factor = 0.2 * math.sqrt(max(M, N))
     back_rows = lax.all_to_all(columns, "tensor", split_axis=0, concat_axis=1, tiled=True)
     scaled = (factor * back_rows.astype(jnp.float32)).astype(jnp.bfloat16)
-    every_slot = lax.all_gather(scaled[None], "dp", axis=0, tiled=True)
+    every_slot = gather_around(scaled[None], "dp", 0)
     matrix_ids = jnp.arange(every_slot.shape[0], dtype=jnp.int32)
     selector = (owner[None, :] == matrix_ids[:, None]).astype(jnp.bfloat16)
     update = jnp.einsum(

time: 287 us -> 330 us (1.15); the launches traced: 287 us -> 325 us
  local copies, waits for them, and re-layouts: 6.44 us -> 62.1 us
  between operations: 14.8 us -> 1.47 us
  waiting for transfers between devices: 28.5 us -> 23.8 us
    concatenate x0 -> x1, local copies, waits for them, and re-layouts: none -> 43 us  [gather_around(): jnp.roll(line, (lax.axis_index(axis) - ways // 2) * x.shape[dim], axis=dim)]
    all_gather x1 -> x0, waiting for transfers between devices: 28.5 us -> none  [per_device(): every_slot = lax.all_gather(scaled[None], 'dp', axis=0, tiled=True)]
    ppermute x0 -> x3, waiting for transfers between devices: none -> 23.8 us  [the longest x2 23.8 us: gather_around(): earlier.append(lax.ppermute(earlier[-1], axis, up))]
    ppermute x0 -> x3, local copies, waits for them, and re-layouts: none -> 10.1 us  [the longest x2 6.27 us: gather_around(): earlier.append(lax.ppermute(earlier[-1], axis, up))]
  transfers between devices with their start and end apart: 1 -> 3, of which waited for: 1 -> 2; matrix products, arithmetic and copies ran while one was open for 0% -> 3% of each run, Pallas kernels for 0% -> 0%
where the time goes in v1:
time: 330 us; the launch traced here: 325 us
  blocking collectives  222 us (67%)
  local copies, waits for them, and re-layouts  62.1 us (19%)
  waiting for transfers between devices  23.8 us (7%)
  matrix products  10.2 us (3%)
    psum x2, blocking collectives, per_device(): lax.psum(jnp.dot(columns, columns.T, preferred_element_type=jnp.float32),...  160 us
    concatenate x1, local copies, waits for them, and re-layouts, gather_around(): jnp.roll(line, (lax.axis_index(axis) - ways // 2) * x.shape[dim], axis=dim)  43 us
    psum x1, blocking collectives, per_device(): total = lax.psum(jnp.sum(direction * direction), 'tensor')  23.8 us
    ppermute x2, waiting for transfers between devices, gather_around(): earlier.append(lax.ppermute(earlier[-1], axis, up))  23.8 us
    all_to_all x1, blocking collectives, per_device(): lax.all_to_all(rows_here, 'tensor', split_axis=1, concat_axis=0, tiled=True)  21.7 us
    all_to_all x1, blocking collectives, per_device(): lax.all_to_all(columns, 'tensor', split_axis=0, concat_axis=1, tiled=True)  17.1 us
  transfers between devices with their start and end apart: 3, of which 2 were waited for; matrix products, arithmetic and copies ran while one was open for 3% of the time, Pallas kernels for 0%

profile of v1, /device:TPU:0, one launch (start us, length us, event | category | flops | bytes accessed | tf_op | source)
XLA Modules:
  0.0 324.6 jit_solution(15238831439382099425)
XLA Ops:
  0.6 0.0 copy-start.1
  0.6 2.9 multiply_reduce_fusion
  3.5 0.0 copy-start
  3.5 23.8 %psum.21 = f32[]{:T(128)} all-reduce(f32[]{:T(128)} %get-tuple-element.8), channel_id=1, replica_groups=mesh['dp'=4,'tensor'=8] {'tensor'}, use_global_device_ids=true, to_apply=%region_1.0 | all-reduce | flops 1 | bytes 8 | tf_op jit(solution)/shard_map/psum | solution.py:33
  28.0 0.0 copy-done.1
  28.0 0.3 divide_convert_fusion
  28.3 0.0 copy-done
  28.3 0.2 copy.26
  28.4 0.2 copy.15
  28.6 21.7 %all_to_all.29 = bf16[72,8,768]{2,0,1:T(8,128)(2,1)S(1)} all-to-all(bf16[72,8,768]{2,0,1:T(8,128)(2,1)S(1)} %copy.15), channel_id=1, replica_groups=mesh['dp'=4,'tensor'=8] {'tensor'}, dimensions={1} | all-to-all | bytes 1769472 | tf_op jit(solution)/shard_map/all_to_all | solution.py:35
  50.3 0.9 fusion.18
  51.2 80.3 %all-reduce.2 = bf16[576,576]{1,0:T(8,128)(2,1)S(1)} all-reduce(f32[576,576]{1,0:T(8,128)S(1)} %fusion.18), channel_id=1, replica_groups=mesh['dp'=4,'tensor'=8] {'tensor'}, use_global_device_ids=true, to_apply=%region_2.0 | all-reduce | flops 331776 | bytes 1990656 | tf_op jit(solution)/shard_map/psum | solution.py:37
  131.5 1.6 add_convert_fusion.1
  133.1 0.0 copy-start.3
  133.1 0.9 copy-done.3
  134.0 0.9 fusion.19
  134.9 0.0 copy-start.4
  134.9 79.2 %all-reduce.3 = bf16[576,576]{1,0:T(8,128)(2,1)S(1)} all-reduce(f32[576,576]{1,0:T(8,128)S(1)} %fusion.19), channel_id=1, replica_groups=mesh['dp'=4,'tensor'=8] {'tensor'}, use_global_device_ids=true, to_apply=%region_3.0 | all-reduce | flops 331776 | bytes 1990656 | tf_op jit(solution)/shard_map/psum | solution.py:37
  214.1 0.0 copy-done.4
  214.1 1.6 add_convert_fusion
  215.8 17.1 %all_to_all.30 = bf16[8,72,768]{2,1,0:T(8,128)(2,1)S(1)} all-to-all(bf16[8,72,768]{2,1,0:T(8,128)(2,1)S(1)} %bitcast.26), channel_id=1, replica_groups=mesh['dp'=4,'tensor'=8] {'tensor'}, dimensions={0} | all-to-all | bytes 1769472 | tf_op jit(solution)/shard_map/all_to_all | solution.py:45
  232.9 0.2 fusion.1
  233.0 0.2 copy.16
  233.2 1.3 convert_element_type.89
  234.5 0.0 collective-permute-start
  234.5 1.7 collective-permute-start.2
  236.3 19.9 %collective-permute-done = bf16[1,72,6144]{2,1,0:T(8,128)(2,1)} collective-permute-done((bf16[1,72,6144]{2,1,0:T(8,128)(2,1)}, bf16[1,72,6144]{2,1,0:T(8,128)(2,1)}, u32[]{:S(2)}, u32[]{:S(2)}) %collective-permute-start) | collective-permute-done | bytes 884768 | tf_op jit(solution)/shard_map/ppermute | solution.py:23
  256.1 0.0 collective-permute-start.1
  256.1 2.5 copy.19
  258.7 2.5 copy.18
  261.2 0.0 collective-permute-done.2
  261.2 3.8 %copy.20 = bf16[1,72,6144]{2,0,1:T(2,128)(2,1)} copy(bf16[1,72,6144]{2,1,0:T(8,128)(2,1)} %collective-permute-done.2) | data formatting | bytes 1769472 | tf_op jit(solution)/shard_map/ppermute | solution.py:25
  265.1 3.9 %collective-permute-done.1 = bf16[1,72,6144]{2,1,0:T(8,128)(2,1)} collective-permute-done((bf16[1,72,6144]{2,1,0:T(8,128)(2,1)}, bf16[1,72,6144]{2,1,0:T(8,128)(2,1)}, u32[]{:S(2)}, u32[]{:S(2)}) %collective-permute-start.1) | collective-permute-done | bytes 884768 | tf_op jit(solution)/shard_map/ppermute | solution.py:23
  268.9 3.7 %copy.17 = bf16[1,72,6144]{2,0,1:T(2,128)(2,1)} copy(bf16[1,72,6144]{2,1,0:T(8,128)(2,1)} %collective-permute-done.1) | data formatting | bytes 1769472 | tf_op jit(solution)/shard_map/ppermute | solution.py:23
  272.7 0.0 copy-start.2
  272.7 43.0 %concatenate.6 = bf16[8,72,6144]{2,0,1:T(8,128)(2,1)} concatenate(bf16[1,72,6144]{2,0,1:T(2,128)(2,1)} %copy.17, bf16[1,72,6144]{2,0,1:T(2,128)(2,1)S(1)} %copy.18, bf16[1,72,6144]{2,0,1:T(2,128)(2,1)S(1)} %copy.19, bf16[1,72,6144]{2,0,1:T(2,128)(2,1)} %copy.20, bf16[1,72,6144]{2,0,1:T(2,128)(2,1)} %copy.17, bf16[1,72,6144]{2,0,1:T(2,128)(2,1)S(1)} %copy.18, ...), dimensions={0} | concatenate | bytes 14155776 | tf_op jit(solution)/shard_map/jit(_roll_dynamic)/concatenate | solution.py:27
  315.7 0.0 copy-done.2
  315.7 5.2 %convolution_convert_fusion = bf16[4,72,6144]{2,0,1:T(4,128)(2,1)S(1)} fusion(bf16[8,72,6144]{2,0,1:T(8,128)(2,1)} %concatenate.6, s32[]{:T(128)S(6)} %select_n.14, s32[4]{0:T(128)S(1)} %copy-done.2), kind=kOutput, calls=%fused_computation | convolution fusion | flops 15925264 | bytes 7077908 | tf_op jit(solution)/shard_map/mg,grn->mrn/dot_general | solution.py:50
  320.9 3.7 %copy.25 = bf16[4,72,6144]{2,1,0:T(8,128)(2,1)} copy(bf16[4,72,6144]{2,0,1:T(4,128)(2,1)S(1)} %convolution_convert_fusion) | data formatting | bytes 7077888
Async XLA Ops:
  0.6 27.4 %copy-start.1 = (bf16[1,72,6144]{2,1,0:T(8,128)(2,1)S(1)}, bf16[1,72,6144]{2,1,0:T(8,128)(2,1)}, u32[]{:S(2)}) copy-start(bf16[1,72,6144]{2,1,0:T(8,128)(2,1)} %param.3) | copy-start | bytes 2654212
  3.5 24.7 %copy-start = (f32[1,72,6144]{2,1,0:T(8,128)}, f32[1,72,6144]{2,1,0:T(8,128)S(1)}, u32[]{:S(2)}) copy-start(f32[1,72,6144]{2,1,0:T(8,128)S(1)} %get-tuple-element.9) | copy-start | bytes 5308420
  133.1 0.9 copy-start.3
  134.9 79.2 %copy-start.4 = (bf16[576,768]{1,0:T(8,128)(2,1)S(1)}, bf16[576,768]{1,0:T(8,128)(2,1)}, u32[]{:S(2)}) copy-start(bf16[576,768]{1,0:T(8,128)(2,1)} %copy-done.3) | copy-start | bytes 2654212
  234.5 21.6 %collective-permute-start = (bf16[1,72,6144]{2,1,0:T(8,128)(2,1)}, bf16[1,72,6144]{2,1,0:T(8,128)(2,1)}, u32[]{:S(2)}, u32[]{:S(2)}) collective-permute-start(bf16[1,72,6144]{2,1,0:T(8,128)(2,1)} %convert_element_type.89), channel_id=1, source_target_pairs={{0,8},{8,16},{16,24},{24,0},{1,9},{9,17},{17,25},{25,1},{2,10},{10... | collective-permute-start | bytes 2654216 | tf_op jit(solution)/shard_map/ppermute | solution.py:23
  234.5 26.7 %collective-permute-start.2 = (bf16[1,72,6144]{2,1,0:T(8,128)(2,1)}, bf16[1,72,6144]{2,1,0:T(8,128)(2,1)}, u32[]{:S(2)}, u32[]{:S(2)}) collective-permute-start(bf16[1,72,6144]{2,1,0:T(8,128)(2,1)} %convert_element_type.89), channel_id=1, source_target_pairs={{0,24},{8,0},{16,8},{24,16},{1,25},{9,1},{17,9},{25,17},{2,26},{10... | collective-permute-start | bytes 2654216 | tf_op jit(solution)/shard_map/ppermute | solution.py:25
  256.1 12.8 %collective-permute-start.1 = (bf16[1,72,6144]{2,1,0:T(8,128)(2,1)}, bf16[1,72,6144]{2,1,0:T(8,128)(2,1)}, u32[]{:S(2)}, u32[]{:S(2)}) collective-permute-start(bf16[1,72,6144]{2,1,0:T(8,128)(2,1)} %collective-permute-done), channel_id=1, source_target_pairs={{0,8},{8,16},{16,24},{24,0},{1,9},{9,17},{17,25},{25,1},{2,10},{10... | collective-permute-start | bytes 2654216 | tf_op jit(solution)/shard_map/ppermute | solution.py:23
  272.7 43.0 %copy-start.2 = (s32[4]{0:T(128)S(1)}, s32[4]{0:T(128)}, u32[]{:S(2)}) copy-start(s32[4]{0:T(128)} %param.5) | copy-start | bytes 52
